TPU v7x, 512 devices: a whole 4x4x16 slice. The times are simulated.
512 devices in a mesh: tile: 64 (over z, x_hi, core), chan: 8 (over x_lo, y).
Axes of the slice: x: 4 (x_hi: 2, x_lo: 2; x = x_hi * 2 + x_lo), y: 4, z: 16, core: 2. Of those that a mesh axis runs over, the one named last changes fastest.
Arguments:
- analysis: bfloat16 [64, 524288], P('chan', 'tile'), may hold values from -6 to 6
- send_rows: int32 [64, 5, 128], P('tile'), may hold values from 0 to 8191
- send_count: int32 [64, 5], P('tile'), may hold values from 64 to 128, as said below
- corner_slot: int32 [4, 2048, 256], P(None, 'tile'), may hold values from 0 to 639, as said below
- corner_weight: float32 [4, 2048, 256], P(None, 'tile'), may hold values from 0.1 to 0.6
- beside: int32 [2048, 8], P('tile'), may hold values from 0 to 2047, as said below
- quarter_turns: int32 [2048, 8], P('tile'), may hold values from 0 to 3
- kernel_one: bfloat16 [9, 128, 64], P(None, 'chan'), may hold values from -0.375 to 0.375
- kernel_two: bfloat16 [9, 128, 128], P(None, 'chan'), may hold values from -0.25 to 0.25
- kernel_three: bfloat16 [9, 128, 128], P(None, 'chan'), may hold values from -0.25 to 0.25
Outputs:
- forecast: bfloat16 [128, 2048, 256], P('chan', 'tile')
Inputs may be any that keep to these rules, and one draw needn't show every extreme that they name: send_count[s, d] is at least 64; every shard sends 128 to itself (d = 2), and some receiver gets 128 from each of its 5 senders. corner_slot[j, t, i] = d * 128 + k names a live slot, k < send_count[s, d], of the block that shard s = (e - d + 2) mod the shard count sends to the shard e holding tile t; the four corners of a pixel are slots k, k + 1, k + 2, k + 3 of one block. beside[t, k] = (t + d) mod 2048 with 1 <= |d| <= 2.
All inputs are finite; a program needn't handle non-finite values.
Results may differ from a plain program's by a relative error of at most 0.007.
Values may be sent and summed in bfloat16 or wider, within the bound.
No kernel may reach another device: no remote copies, remote signals or barrier semaphores. Data moves between devices by JAX's collectives and lax.ppermute only.
A program may use at most 64 MiB of HBM per device.

v0:
```python
import jax
import jax.numpy as jnp
import numpy as np
from jax import lax
from jax.sharding import PartitionSpec as P

P_SIZE = 16
REACH = 2


def from_behind(value, axis, steps):
    count = lax.axis_size(axis)
    pairs = [(source, (source + steps) % count) for source in range(count)]
    return lax.ppermute(value, axis, pairs)


def extended_2(x, sides, width):
    for axis, dim in sides:
        size, length = (lax.axis_size(axis), x.shape[dim])
        up = [(i, (i + 1) % size) for i in range(size)]
        down = [(j, i) for i, j in up]
        last = lax.slice_in_dim(x, length - width, length, axis=dim)
        initial = lax.slice_in_dim(x, 0, width, axis=dim)
        before = lax.ppermute(last, axis, up)
        after = lax.ppermute(initial, axis, down)
        x = jnp.concatenate([before, x, after], axis=dim)
    return x


def cycle_table(extent):
    length = 4 * extent - 4
    entries = []
    for cycle_pos in range(length):
        if cycle_pos < extent:
            row_at, col_at = (cycle_pos, 0)
        elif cycle_pos < 2 * extent - 1:
            row_at, col_at = (extent - 1, cycle_pos - extent + 1)
        elif cycle_pos < 3 * extent - 2:
            row_at, col_at = (3 * extent - 3 - cycle_pos, extent - 1)
        else:
            row_at, col_at = (0, 4 * extent - 4 - cycle_pos)
        entries.append(row_at * extent + col_at)
    return np.array(entries, np.int32)


def border_tables(extent):
    length = 4 * extent - 4
    heading = []
    anchor = []
    for col_at in range(extent):
        heading.append(0)
        anchor.append(extent - 1 + col_at)
    for col_at in range(extent):
        heading.append(1)
        anchor.append((length - col_at) % length)
    for row_at in range(extent):
        heading.append(2)
        anchor.append(3 * extent - 3 - row_at)
    for row_at in range(extent):
        heading.append(3)
        anchor.append(row_at)
    heading += [4, 5, 6, 7]
    anchor += [2 * extent - 2, extent - 1, 3 * extent - 3, 0]
    return (np.array(heading, np.int32), np.array(anchor, np.int32))


def layout_table(extent):
    padded_side = extent + 2
    interior = extent * extent
    entries = []
    for row_at in range(padded_side):
        for col_at in range(padded_side):
            if 1 <= row_at <= extent and 1 <= col_at <= extent:
                entries.append((row_at - 1) * extent + col_at - 1)
            elif row_at == 0 and 1 <= col_at <= extent:
                entries.append(interior + col_at - 1)
            elif row_at == padded_side - 1 and 1 <= col_at <= extent:
                entries.append(interior + extent + col_at - 1)
            elif col_at == 0 and 1 <= row_at <= extent:
                entries.append(interior + 2 * extent + row_at - 1)
            elif col_at == padded_side - 1 and 1 <= row_at <= extent:
                entries.append(interior + 3 * extent + row_at - 1)
            else:
                corner = (0 if row_at == 0 else 2) + (0 if col_at == 0 else 1)
                entries.append(interior + 4 * extent + corner)
    return np.array(entries, np.int32)


def conv_layer(activity, kernel, local_beside, local_turns, gather_rims):
    length = 4 * P_SIZE - 4
    cycle_vals = jnp.take(activity, cycle_table(P_SIZE), axis=2)
    extended = gather_rims(cycle_vals)
    heading, anchor = border_tables(P_SIZE)
    near_tile = jnp.take(local_beside, heading, axis=1)
    near_turn = jnp.take(local_turns, heading, axis=1)
    source = near_tile * length + jnp.remainder(anchor[None, :] - near_turn * (P_SIZE - 1), length)
    flat_cycles = extended.reshape(extended.shape[0], -1)
    border = jnp.take(flat_cycles, source.reshape(-1), axis=1)
    border = border.reshape(activity.shape[0], activity.shape[1], 4 * P_SIZE + 4)
    joined = jnp.concatenate([activity, border], axis=2)
    padded = jnp.take(joined, layout_table(P_SIZE), axis=2)
    padded_side = P_SIZE + 2
    stretch = P_SIZE * padded_side - 2
    summed = None
    for tap_index in range(9):
        offset = padded_side + 1 + (tap_index // 3 - 1) * padded_side + (tap_index % 3 - 1)
        window = padded[:, :, offset : offset + stretch]
        partial_sum = jnp.einsum(
            "oc,ctq->otq", kernel[tap_index], window, preferred_element_type=jnp.float32
        )
        summed = partial_sum if summed is None else summed + partial_sum
    summed = jnp.pad(summed, ((0, 0), (0, 0), (0, 2)))
    summed = summed.reshape(summed.shape[0], summed.shape[1], P_SIZE, padded_side)[:, :, :, :P_SIZE]
    summed = summed.reshape(summed.shape[0], summed.shape[1], P_SIZE * P_SIZE)
    return jax.nn.gelu(summed, approximate=False).astype(jnp.bfloat16)


def on_device(
    analysis,
    send_rows,
    send_count,
    corner_slot,
    corner_weight,
    beside,
    quarter_turns,
    kernel_one,
    kernel_two,
    kernel_three,
):
    shards = lax.axis_size("tile")
    groups = lax.axis_size("chan")
    tiles_here = corner_slot.shape[1]
    near_count = send_rows.shape[1]
    capacity = send_rows.shape[2]
    channels_here = analysis.shape[0]
    pixels = corner_slot.shape[2]
    total_tiles = tiles_here * shards
    per_group = tiles_here // groups
    widths = [kernel_one.shape[2], kernel_two.shape[2], kernel_three.shape[2]]
    joined_kernels = jnp.concatenate([kernel_one, kernel_two, kernel_three], axis=2)
    joined_kernels = lax.all_gather(joined_kernels, "chan", axis=1, tiled=True)
    kernels = []
    low = 0
    for width in widths:
        kernels.append(joined_kernels[:, :, low : low + width])
        low += width
    slot_order = jnp.arange(capacity)
    rows_list = send_rows[0].reshape(-1)
    piece = jnp.take(analysis, rows_list, axis=1).reshape(channels_here, near_count, capacity)
    is_live = slot_order[None, :] < send_count[0][:, None]
    piece = jnp.where(is_live[None], piece, jnp.zeros((), piece.dtype))
    blocks = []
    for offset_index in range(near_count):
        block = piece[:, offset_index]
        if offset_index != REACH:
            block = from_behind(block, "tile", offset_index - REACH)
        blocks.append(block)
    arrived = jnp.stack(blocks, axis=1).reshape(channels_here, near_count * capacity)
    arrived = lax.all_gather(arrived, "chan", axis=0, tiled=True)
    group_index = lax.axis_index("chan")
    my_slots = lax.dynamic_slice_in_dim(corner_slot, group_index * per_group, per_group, 1)
    my_weights = lax.dynamic_slice_in_dim(corner_weight, group_index * per_group, per_group, 1)
    my_slots = my_slots.reshape(my_slots.shape[0], per_group * pixels)
    my_weights = my_weights.reshape(my_weights.shape[0], per_group * pixels)
    slot_ids = jnp.arange(near_count * capacity)
    summed = None
    for corner in range(my_slots.shape[0]):
        one_hot = (slot_ids[:, None] == my_slots[corner][None, :]).astype(arrived.dtype)
        picked = jnp.dot(arrived, one_hot, preferred_element_type=jnp.float32)
        term = picked * my_weights[corner][None, :]
        summed = term if summed is None else summed + term
    activity = summed.astype(jnp.bfloat16).reshape(arrived.shape[0], per_group, pixels)
    first_tile = lax.axis_index(("tile", "chan")) * per_group
    near_beside = lax.dynamic_slice_in_dim(beside, group_index * per_group, per_group, 0)
    near_turns = lax.dynamic_slice_in_dim(quarter_turns, group_index * per_group, per_group, 0)
    local_beside = jnp.remainder(near_beside - first_tile + REACH, total_tiles)

    def joined_rims(cycle_vals):
        return extended_2(cycle_vals, ((("tile", "chan"), 1),), REACH)

    for kernel in kernels:
        activity = conv_layer(activity, kernel, local_beside, near_turns, joined_rims)
    result = lax.all_to_all(activity, "chan", split_axis=0, concat_axis=1, tiled=True)
    return result


def solution(mesh):
    return jax.shard_map(
        on_device,
        mesh=mesh,
        in_specs=(
            P("chan", "tile"),
            P("tile", None, None),
            P("tile", None),
            P(None, "tile", None),
            P(None, "tile", None),
            P("tile", None),
            P("tile", None),
            P(None, "chan", None),
            P(None, "chan", None),
            P(None, "chan", None),
        ),
        out_specs=P("chan", "tile", None),
        check_vma=False,
    )
```

profile of v0, /device:TPU:2, one launch (start us, length us, event | category | flops | bytes accessed | tf_op | source)
XLA Modules:
  0.0 177.2 jit_solution(4643471819461875339)
XLA Ops:
  0.1 0.8 fusion.74
  0.8 0.8 iota_compare_fusion.24
  1.6 1.9 %copy.243 = bf16[8,8192]{0,1:T(8,128)(2,1)S(1)} copy(bf16[8,8192]{1,0:T(8,128)(2,1)} %param.30) | data formatting | bytes 262144 | tf_op args[0]
  3.5 2.0 %gather_fusion = bf16[640,8]{1,0:T(8,128)(2,1)S(1)} fusion(bf16[8,8192]{0,1:T(8,128)(2,1)S(1)} %copy.243, s32[1024]{0:T(1024)S(1)} %pad_clamp_fusion.5), kind=kCustom, calls=%fused_computation.8 | custom fusion | bytes 23040 | tf_op jit(solution)/shard_map/jit(_take)/gather | solution.py:149
  5.6 13.0 %collective-permute-start = (bf16[8,128]{1,0:T(8,128)(2,1)S(1)}, bf16[8,128]{1,0:T(8,128)(2,1)S(1)}, u32[]{:S(2)}, u32[]{:S(2)}) collective-permute-start(bf16[8,128]{1,0:T(8,128)(2,1)S(1)} %get-tuple-element.35), channel_id=1, source_target_pairs={{0,496},{8,504},{16,0},{24,8},{32,16},{40,24},{48,32},{56,40},{64,... | collective-permute-start | bytes 6152 | tf_op jit(solution)/shard_map/ppermute | solution.py:14
  18.6 2.5 %collective-permute-start.1 = (bf16[8,128]{1,0:T(8,128)(2,1)S(1)}, bf16[8,128]{1,0:T(8,128)(2,1)S(1)}, u32[]{:S(2)}, u32[]{:S(2)}) collective-permute-start(bf16[8,128]{1,0:T(8,128)(2,1)S(1)} %get-tuple-element.34), channel_id=1, source_target_pairs={{0,504},{8,0},{16,8},{24,16},{32,24},{40,32},{48,40},{56,48},{64,5... | collective-permute-start | bytes 6152 | tf_op jit(solution)/shard_map/ppermute | solution.py:14
  24.5 29.9 %all_gather.6 = bf16[9,128,320]{2,1,0:T(8,128)(2,1)S(1)} all-gather(bf16[9,16,320]{2,1,0:T(8,128)(2,1)S(1)} %pad_maximum_fusion.6), channel_id=1, replica_groups=mesh['tile'=64,'chan'=8] {'chan'}, dimensions={1}, use_global_device_ids=true | all-gather | bytes 829440 | tf_op jit(solution)/shard_map/all_gather | solution.py:141
  54.5 1.9 %collective-permute-start.2 = (bf16[8,128]{1,0:T(8,128)(2,1)S(1)}, bf16[8,128]{1,0:T(8,128)(2,1)S(1)}, u32[]{:S(2)}, u32[]{:S(2)}) collective-permute-start(bf16[8,128]{1,0:T(8,128)(2,1)S(1)} %get-tuple-element.32), channel_id=1, source_target_pairs={{0,8},{8,16},{16,24},{24,32},{32,40},{40,48},{48,56},{56,64},{64,7... | collective-permute-start | bytes 6152 | tf_op jit(solution)/shard_map/ppermute | solution.py:14
  56.6 3.5 %collective-permute-start.3 = (bf16[8,128]{1,0:T(8,128)(2,1)S(1)}, bf16[8,128]{1,0:T(8,128)(2,1)S(1)}, u32[]{:S(2)}, u32[]{:S(2)}) collective-permute-start(bf16[8,128]{1,0:T(8,128)(2,1)S(1)} %get-tuple-element.31), channel_id=1, source_target_pairs={{0,16},{8,24},{16,32},{24,40},{32,48},{40,56},{48,64},{56,72},{64,... | collective-permute-start | bytes 6152 | tf_op jit(solution)/shard_map/ppermute | solution.py:14
  60.1 2.9 %collective-permute-done.2 = bf16[8,128]{1,0:T(8,128)(2,1)S(1)} collective-permute-done((bf16[8,128]{1,0:T(8,128)(2,1)S(1)}, bf16[8,128]{1,0:T(8,128)(2,1)S(1)}, u32[]{:S(2)}, u32[]{:S(2)}) %collective-permute-start.2) | collective-permute-done | bytes 2080 | tf_op jit(solution)/shard_map/ppermute | solution.py:14
  63.1 2.6 %collective-permute-done.3 = bf16[8,128]{1,0:T(8,128)(2,1)S(1)} collective-permute-done((bf16[8,128]{1,0:T(8,128)(2,1)S(1)}, bf16[8,128]{1,0:T(8,128)(2,1)S(1)}, u32[]{:S(2)}, u32[]{:S(2)}) %collective-permute-start.3) | collective-permute-done | bytes 2080 | tf_op jit(solution)/shard_map/ppermute | solution.py:14
  65.7 28.2 %all_gather.7 = bf16[64,640]{1,0:T(8,128)(2,1)S(1)} all-gather(bf16[8,640]{1,0:T(8,128)(2,1)S(1)} %bitcast.272), channel_id=1, replica_groups=mesh['tile'=64,'chan'=8] {'chan'}, dimensions={0}, use_global_device_ids=true | all-gather | bytes 92160 | tf_op jit(solution)/shard_map/all_gather | solution.py:159
  97.3 3.2 %collective-permute-start.4 = (bf16[64,2,60]{0,1,2:T(2,128)(2,1)S(1)}, bf16[64,2,60]{0,1,2:T(2,128)(2,1)S(1)}, u32[]{:S(2)}, u32[]{:S(2)}) collective-permute-start(bf16[64,2,60]{0,1,2:T(2,128)(2,1)S(1)} %get-tuple-element.29), channel_id=1, source_target_pairs={{0,1},{1,2},{2,3},{3,4},{4,5},{5,6},{6,7},{7,8},{8,9},{9,10},{10,1... | collective-permute-start | bytes 46088 | tf_op jit(solution)/shard_map/ppermute | solution.py:24
  100.6 4.9 %collective-permute-start.5 = (bf16[64,2,60]{0,1,2:T(2,128)(2,1)S(1)}, bf16[64,2,60]{0,1,2:T(2,128)(2,1)S(1)}, u32[]{:S(2)}, u32[]{:S(2)}) collective-permute-start(bf16[64,2,60]{0,1,2:T(2,128)(2,1)S(1)} %get-tuple-element.30), channel_id=1, source_target_pairs={{1,0},{2,1},{3,2},{4,3},{5,4},{6,5},{7,6},{8,7},{9,8},{10,9},{11,1... | collective-permute-start | bytes 46088 | tf_op jit(solution)/shard_map/ppermute | solution.py:25
  105.7 1.2 collective-permute-done.5
  107.1 1.4 gather_fusion.2
  108.9 2.0 %gather_fusion.3 = bf16[324,64,4]{1,2,0:T(4,128)(2,1)S(1)} fusion(bf16[64,4,324]{0,1,2:T(4,128)(2,1)S(1)} %pad_maximum_fusion.2, s32[1024]{0:T(1024)S(1)} %get-tuple-element.37), kind=kCustom, calls=%fused_computation.11 | custom fusion | bytes 333072 | tf_op jit(solution)/shard_map/jit(_take)/gather | solution.py:101
  116.9 1.1 fusion.18
  118.9 2.6 %collective-permute-start.6 = (bf16[128,2,60]{0,1,2:T(2,128)(2,1)S(1)}, bf16[128,2,60]{0,1,2:T(2,128)(2,1)S(1)}, u32[]{:S(2)}, u32[]{:S(2)}) collective-permute-start(bf16[128,2,60]{0,1,2:T(2,128)(2,1)S(1)} %get-tuple-element.27), channel_id=1, source_target_pairs={{0,1},{1,2},{2,3},{3,4},{4,5},{5,6},{6,7},{7,8},{8,9},{9,10},{10,1... | collective-permute-start | bytes 92168 | tf_op jit(solution)/shard_map/ppermute | solution.py:24
  121.5 5.9 %collective-permute-start.7 = (bf16[128,2,60]{0,1,2:T(2,128)(2,1)S(1)}, bf16[128,2,60]{0,1,2:T(2,128)(2,1)S(1)}, u32[]{:S(2)}, u32[]{:S(2)}) collective-permute-start(bf16[128,2,60]{0,1,2:T(2,128)(2,1)S(1)} %get-tuple-element.28), channel_id=1, source_target_pairs={{1,0},{2,1},{3,2},{4,3},{5,4},{6,5},{7,6},{8,7},{9,8},{10,9},{11,1... | collective-permute-start | bytes 92168 | tf_op jit(solution)/shard_map/ppermute | solution.py:25
  127.4 1.3 collective-permute-done.7
  128.9 1.4 gather_fusion.7
  130.9 2.0 %gather_fusion.8 = bf16[324,128,4]{1,2,0:T(4,128)(2,1)S(1)} fusion(bf16[128,4,324]{0,1,2:T(4,128)(2,1)S(1)} %copy.275, s32[1024]{0:T(1024)S(1)} %get-tuple-element.37), kind=kCustom, calls=%fused_computation.3.clone | custom fusion | bytes 664848 | tf_op jit(solution)/shard_map/jit(_take)/gather | solution.py:101
  137.0 1.1 fusion.21
  139.0 2.5 %collective-permute-start.8 = (bf16[128,2,60]{0,1,2:T(2,128)(2,1)S(1)}, bf16[128,2,60]{0,1,2:T(2,128)(2,1)S(1)}, u32[]{:S(2)}, u32[]{:S(2)}) collective-permute-start(bf16[128,2,60]{0,1,2:T(2,128)(2,1)S(1)} %get-tuple-element.25), channel_id=1, source_target_pairs={{0,1},{1,2},{2,3},{3,4},{4,5},{5,6},{6,7},{7,8},{8,9},{9,10},{10,1... | collective-permute-start | bytes 92168 | tf_op jit(solution)/shard_map/ppermute | solution.py:24
  141.5 5.8 %collective-permute-start.9 = (bf16[128,2,60]{0,1,2:T(2,128)(2,1)S(1)}, bf16[128,2,60]{0,1,2:T(2,128)(2,1)S(1)}, u32[]{:S(2)}, u32[]{:S(2)}) collective-permute-start(bf16[128,2,60]{0,1,2:T(2,128)(2,1)S(1)} %get-tuple-element.26), channel_id=1, source_target_pairs={{1,0},{2,1},{3,2},{4,3},{5,4},{6,5},{7,6},{8,7},{9,8},{10,9},{11,1... | collective-permute-start | bytes 92168 | tf_op jit(solution)/shard_map/ppermute | solution.py:25
  147.3 1.5 collective-permute-done.9
  149.0 1.4 gather_fusion.10
  151.0 2.0 %gather_fusion.11 = bf16[324,128,4]{1,2,0:T(4,128)(2,1)S(1)} fusion(bf16[128,4,324]{0,1,2:T(4,128)(2,1)S(1)} %copy.289, s32[1024]{0:T(1024)S(1)} %get-tuple-element.37), kind=kCustom, calls=%fused_computation.7.clone | custom fusion | bytes 664848 | tf_op jit(solution)/shard_map/jit(_take)/gather | solution.py:101
  157.2 1.1 fusion.24
  158.5 17.9 %all_to_all.18 = bf16[128,4,256]{2,1,0:T(4,128)(2,1)S(1)} all-to-all(bf16[128,4,256]{2,1,0:T(4,128)(2,1)S(1)} %copy.300), channel_id=1, replica_groups=mesh['tile'=64,'chan'=8] {'chan'}, dimensions={0} | all-to-all | bytes 524288 | tf_op jit(solution)/shard_map/all_to_all | solution.py:183
  176.4 0.8 copy.303
  (146 shorter events, 25.2 us)
Async XLA Ops:
  0.0 21.9 %copy-start = (s32[32,8]{0,1:T(8,128)S(1)}, s32[32,8]{0,1:T(8,128)}, u32[]{:S(2)}) copy-start(s32[32,8]{0,1:T(8,128)} %param.36) | copy-start | bytes 3076
  0.0 21.1 %copy-start.7 = (s32[68]{0:T(128)S(1)}, s32[68]{0:T(128)}, u32[]{:S(2)}) copy-start(s32[68]{0:T(128)} %constant.310) | copy-start | bytes 820
  0.0 22.7 %copy-start.6 = (s32[68]{0:T(128)S(1)}, s32[68]{0:T(128)}, u32[]{:S(2)}) copy-start(s32[68]{0:T(128)} %constant.243) | copy-start | bytes 820
  0.0 56.5 %copy-start.8 = (s32[60]{0:T(128)S(1)}, s32[60]{0:T(128)}, u32[]{:S(2)}) copy-start(s32[60]{0:T(128)} %constant.221.clone) | copy-start | bytes 724
  0.0 21.1 %copy-start.4 = (s32[32,8]{0,1:T(8,128)S(1)}, s32[32,8]{0,1:T(8,128)}, u32[]{:S(2)}) copy-start(s32[32,8]{0,1:T(8,128)} %param.35) | copy-start | bytes 3076
  0.0 24.3 %copy-start.3 = (bf16[9,16,64]{2,1,0:T(8,128)(2,1)S(1)}, bf16[9,16,64]{2,1,0:T(8,128)(2,1)}, u32[]{:S(2)}) copy-start(bf16[9,16,64]{2,1,0:T(8,128)(2,1)} %param.37) | copy-start | bytes 55300
  0.0 24.3 %copy-start.2 = (bf16[9,16,128]{2,1,0:T(8,128)(2,1)S(1)}, bf16[9,16,128]{2,1,0:T(8,128)(2,1)}, u32[]{:S(2)}) copy-start(bf16[9,16,128]{2,1,0:T(8,128)(2,1)} %param.38) | copy-start | bytes 110596
  0.1 24.3 %copy-start.1 = (bf16[9,16,128]{2,1,0:T(8,128)(2,1)S(1)}, bf16[9,16,128]{2,1,0:T(8,128)(2,1)}, u32[]{:S(2)}) copy-start(bf16[9,16,128]{2,1,0:T(8,128)(2,1)} %param.39) | copy-start | bytes 110596
  5.6 48.8 %collective-permute-start = (bf16[8,128]{1,0:T(8,128)(2,1)S(1)}, bf16[8,128]{1,0:T(8,128)(2,1)S(1)}, u32[]{:S(2)}, u32[]{:S(2)}) collective-permute-start(bf16[8,128]{1,0:T(8,128)(2,1)S(1)} %get-tuple-element.35), channel_id=1, source_target_pairs={{0,496},{8,504},{16,0},{24,8},{32,16},{40,24},{48,32},{56,40},{64,... | collective-permute-start | bytes 6152 | tf_op jit(solution)/shard_map/ppermute | solution.py:14
  18.6 35.9 %collective-permute-start.1 = (bf16[8,128]{1,0:T(8,128)(2,1)S(1)}, bf16[8,128]{1,0:T(8,128)(2,1)S(1)}, u32[]{:S(2)}, u32[]{:S(2)}) collective-permute-start(bf16[8,128]{1,0:T(8,128)(2,1)S(1)} %get-tuple-element.34), channel_id=1, source_target_pairs={{0,504},{8,0},{16,8},{24,16},{32,24},{40,32},{48,40},{56,48},{64,5... | collective-permute-start | bytes 6152 | tf_op jit(solution)/shard_map/ppermute | solution.py:14
  54.5 8.5 %collective-permute-start.2 = (bf16[8,128]{1,0:T(8,128)(2,1)S(1)}, bf16[8,128]{1,0:T(8,128)(2,1)S(1)}, u32[]{:S(2)}, u32[]{:S(2)}) collective-permute-start(bf16[8,128]{1,0:T(8,128)(2,1)S(1)} %get-tuple-element.32), channel_id=1, source_target_pairs={{0,8},{8,16},{16,24},{24,32},{32,40},{40,48},{48,56},{56,64},{64,7... | collective-permute-start | bytes 6152 | tf_op jit(solution)/shard_map/ppermute | solution.py:14
  56.6 9.1 %collective-permute-start.3 = (bf16[8,128]{1,0:T(8,128)(2,1)S(1)}, bf16[8,128]{1,0:T(8,128)(2,1)S(1)}, u32[]{:S(2)}, u32[]{:S(2)}) collective-permute-start(bf16[8,128]{1,0:T(8,128)(2,1)S(1)} %get-tuple-element.31), channel_id=1, source_target_pairs={{0,16},{8,24},{16,32},{24,40},{32,48},{40,56},{48,64},{56,72},{64,... | collective-permute-start | bytes 6152 | tf_op jit(solution)/shard_map/ppermute | solution.py:14
  94.5 11.0 %copy-start.5 = (s32[324]{0:T(512)S(1)}, s32[324]{0:T(512)}, u32[]{:S(2)}) copy-start(s32[324]{0:T(512)} %constant.224.clone) | copy-start | bytes 3892
  97.3 8.3 %collective-permute-start.4 = (bf16[64,2,60]{0,1,2:T(2,128)(2,1)S(1)}, bf16[64,2,60]{0,1,2:T(2,128)(2,1)S(1)}, u32[]{:S(2)}, u32[]{:S(2)}) collective-permute-start(bf16[64,2,60]{0,1,2:T(2,128)(2,1)S(1)} %get-tuple-element.29), channel_id=1, source_target_pairs={{0,1},{1,2},{2,3},{3,4},{4,5},{5,6},{6,7},{7,8},{8,9},{9,10},{10,1... | collective-permute-start | bytes 46088 | tf_op jit(solution)/shard_map/ppermute | solution.py:24
  100.6 6.3 %collective-permute-start.5 = (bf16[64,2,60]{0,1,2:T(2,128)(2,1)S(1)}, bf16[64,2,60]{0,1,2:T(2,128)(2,1)S(1)}, u32[]{:S(2)}, u32[]{:S(2)}) collective-permute-start(bf16[64,2,60]{0,1,2:T(2,128)(2,1)S(1)} %get-tuple-element.30), channel_id=1, source_target_pairs={{1,0},{2,1},{3,2},{4,3},{5,4},{6,5},{7,6},{8,7},{9,8},{10,9},{11,1... | collective-permute-start | bytes 46088 | tf_op jit(solution)/shard_map/ppermute | solution.py:25
  118.9 8.5 %collective-permute-start.6 = (bf16[128,2,60]{0,1,2:T(2,128)(2,1)S(1)}, bf16[128,2,60]{0,1,2:T(2,128)(2,1)S(1)}, u32[]{:S(2)}, u32[]{:S(2)}) collective-permute-start(bf16[128,2,60]{0,1,2:T(2,128)(2,1)S(1)} %get-tuple-element.27), channel_id=1, source_target_pairs={{0,1},{1,2},{2,3},{3,4},{4,5},{5,6},{6,7},{7,8},{8,9},{9,10},{10,1... | collective-permute-start | bytes 92168 | tf_op jit(solution)/shard_map/ppermute | solution.py:24
  121.5 7.3 %collective-permute-start.7 = (bf16[128,2,60]{0,1,2:T(2,128)(2,1)S(1)}, bf16[128,2,60]{0,1,2:T(2,128)(2,1)S(1)}, u32[]{:S(2)}, u32[]{:S(2)}) collective-permute-start(bf16[128,2,60]{0,1,2:T(2,128)(2,1)S(1)} %get-tuple-element.28), channel_id=1, source_target_pairs={{1,0},{2,1},{3,2},{4,3},{5,4},{6,5},{7,6},{8,7},{9,8},{10,9},{11,1... | collective-permute-start | bytes 92168 | tf_op jit(solution)/shard_map/ppermute | solution.py:25
  139.0 8.3 %collective-permute-start.8 = (bf16[128,2,60]{0,1,2:T(2,128)(2,1)S(1)}, bf16[128,2,60]{0,1,2:T(2,128)(2,1)S(1)}, u32[]{:S(2)}, u32[]{:S(2)}) collective-permute-start(bf16[128,2,60]{0,1,2:T(2,128)(2,1)S(1)} %get-tuple-element.25), channel_id=1, source_target_pairs={{0,1},{1,2},{2,3},{3,4},{4,5},{5,6},{6,7},{7,8},{8,9},{9,10},{10,1... | collective-permute-start | bytes 92168 | tf_op jit(solution)/shard_map/ppermute | solution.py:24
  141.5 7.4 %collective-permute-start.9 = (bf16[128,2,60]{0,1,2:T(2,128)(2,1)S(1)}, bf16[128,2,60]{0,1,2:T(2,128)(2,1)S(1)}, u32[]{:S(2)}, u32[]{:S(2)}) collective-permute-start(bf16[128,2,60]{0,1,2:T(2,128)(2,1)S(1)} %get-tuple-element.26), channel_id=1, source_target_pairs={{1,0},{2,1},{3,2},{4,3},{5,4},{6,5},{7,6},{8,7},{9,8},{10,9},{11,1... | collective-permute-start | bytes 92168 | tf_op jit(solution)/shard_map/ppermute | solution.py:25
where the time goes:
time: 178 us; the launch traced here: 177 us
  blocking collectives  76 us (43%)
  starting transfers between devices  45.7 us (26%)
  local copies, waits for them, and re-layouts  25.4 us (14%)
  matrix products  12.5 us (7%)
  waiting for transfers between devices  9.64 us (5%)
  other arithmetic  6.83 us (4%)
    all_gather x1, blocking collectives, on_device(): joined_kernels = lax.all_gather(joined_kernels, 'chan', axis=1, tiled=True)  29.9 us
    all_gather x1, blocking collectives, on_device(): arrived = lax.all_gather(arrived, 'chan', axis=0, tiled=True)  28.2 us
    ppermute x4, starting transfers between devices, from_behind(): return lax.ppermute(value, axis, pairs)  20.9 us
    all_to_all x1, blocking collectives, on_device(): lax.all_to_all(activity, 'chan', split_axis=0, concat_axis=1, tiled=True)  17.9 us
    ppermute x3, starting transfers between devices, extended_2(): after = lax.ppermute(initial, axis, down)  16.6 us
    dot_general x27, matrix products, conv_layer(): jnp.einsum('oc,ctq->otq', kernel[tap_index], window, preferred_element_ty...  10.1 us
    ppermute x3, starting transfers between devices, extended_2(): before = lax.ppermute(last, axis, up)  8.27 us
    gather x6, local copies, waits for them, and re-layouts, conv_layer(): padded = jnp.take(joined, layout_table(P_SIZE), axis=2)  6.41 us
  transfers between devices with their start and end apart: 10, of which 5 were waited for; matrix products, arithmetic and copies ran while one was open for 2% of the time, Pallas kernels for 0%

commit v1 on v0

--- a/solution.py
+++ b/solution.py
@@ -138,7 +138,9 @@
     per_group = tiles_here // groups
     widths = [kernel_one.shape[2], kernel_two.shape[2], kernel_three.shape[2]]
     joined_kernels = jnp.concatenate([kernel_one, kernel_two, kernel_three], axis=2)
-    joined_kernels = lax.all_gather(joined_kernels, "chan", axis=1, tiled=True)
+    joined_kernels = jnp.concatenate(
+        lax.all_to_all(jnp.stack([joined_kernels] * lax.axis_size("chan")), "chan", 0, 0), axis=1
+    )
     kernels = []
     low = 0
     for width in widths:

time: 178 us -> 155 us (0.87)
  blocking collectives: 76 us -> 45.8 us
  starting transfers between devices: 45.7 us -> 52.2 us
    all_gather x1 -> x0, blocking collectives: 29.9 us -> none  [on_device(): joined_kernels = lax.all_gather(joined_kernels, 'chan', axis=1, tiled=True)]
    all_to_all x0 -> x1, starting transfers between devices: none -> 5.93 us  [on_device(): lax.all_to_all(jnp.stack([joined_kernels] * lax.axis_size('chan')), 'chan...]
  transfers between devices with their start and end apart: 10 -> 11, of which waited for: 5 -> 5; matrix products, arithmetic and copies ran while one was open for 2% -> 8% of each run, Pallas kernels for 0% -> 0%
where the time goes in v1:
time: 155 us; the launch traced here: 154 us
  starting transfers between devices  52.2 us (34%)
  blocking collectives  45.8 us (30%)
  local copies, waits for them, and re-layouts  26.5 us (17%)
  matrix products  12.5 us (8%)
  waiting for transfers between devices  9.13 us (6%)
  other arithmetic  6.81 us (4%)
    all_gather x1, blocking collectives, on_device(): arrived = lax.all_gather(arrived, 'chan', axis=0, tiled=True)  28.2 us
    ppermute x4, starting transfers between devices, from_behind(): return lax.ppermute(value, axis, pairs)  21.4 us
    ppermute x3, starting transfers between devices, extended_2(): after = lax.ppermute(initial, axis, down)  18.1 us
    all_to_all x1, blocking collectives, on_device(): lax.all_to_all(activity, 'chan', split_axis=0, concat_axis=1, tiled=True)  17.6 us
    dot_general x27, matrix products, conv_layer(): jnp.einsum('oc,ctq->otq', kernel[tap_index], window, preferred_element_ty...  10.1 us
    ppermute x3, starting transfers between devices, extended_2(): before = lax.ppermute(last, axis, up)  6.77 us
    gather x6, local copies, waits for them, and re-layouts, conv_layer(): padded = jnp.take(joined, layout_table(P_SIZE), axis=2)  6.41 us
    all_to_all x1, starting transfers between devices, on_device(): lax.all_to_all(jnp.stack([joined_kernels] * lax.axis_size('chan')), 'chan...  5.93 us
  transfers between devices with their start and end apart: 11, of which 5 were waited for; matrix products, arithmetic and copies ran while one was open for 8% of the time, Pallas kernels for 0%

profile of v1, /device:TPU:2, one launch (start us, length us, event | category | flops | bytes accessed | tf_op | source)
XLA Modules:
  0.0 154.0 jit_solution(834901621001761742)
XLA Ops:
  0.8 0.8 iota_compare_fusion.24
  1.5 1.9 %copy.221 = bf16[8,8192]{0,1:T(8,128)(2,1)S(1)} copy(bf16[8,8192]{1,0:T(8,128)(2,1)} %param.30) | data formatting | bytes 262144 | tf_op args[0]
  3.5 2.0 %gather_fusion = bf16[640,8]{1,0:T(8,128)(2,1)S(1)} fusion(bf16[8,8192]{0,1:T(8,128)(2,1)S(1)} %copy.221, s32[1024]{0:T(1024)S(1)} %pad_clamp_fusion.5), kind=kCustom, calls=%fused_computation.8 | custom fusion | bytes 23040 | tf_op jit(solution)/shard_map/jit(_take)/gather | solution.py:151
  5.6 13.0 %collective-permute-start = (bf16[8,128]{1,0:T(8,128)(2,1)S(1)}, bf16[8,128]{1,0:T(8,128)(2,1)S(1)}, u32[]{:S(2)}, u32[]{:S(2)}) collective-permute-start(bf16[8,128]{1,0:T(8,128)(2,1)S(1)} %get-tuple-element.35), channel_id=1, source_target_pairs={{0,496},{8,504},{16,0},{24,8},{32,16},{40,24},{48,32},{56,40},{64,... | collective-permute-start | bytes 6152 | tf_op jit(solution)/shard_map/ppermute | solution.py:14
  18.6 2.5 %collective-permute-start.1 = (bf16[8,128]{1,0:T(8,128)(2,1)S(1)}, bf16[8,128]{1,0:T(8,128)(2,1)S(1)}, u32[]{:S(2)}, u32[]{:S(2)}) collective-permute-start(bf16[8,128]{1,0:T(8,128)(2,1)S(1)} %get-tuple-element.34), channel_id=1, source_target_pairs={{0,504},{8,0},{16,8},{24,16},{32,24},{40,32},{48,40},{56,48},{64,5... | collective-permute-start | bytes 6152 | tf_op jit(solution)/shard_map/ppermute | solution.py:14
  21.2 1.0 stack.12
  22.2 5.9 %all-to-all-start = ((bf16[8,9,16,320]{3,2,1,0:T(8,128)(2,1)}), bf16[8,9,16,320]{3,2,1,0:T(8,128)(2,1)S(1)}, u32[]{:S(2)}, u32[]{:S(2)}) async-start(bf16[8,9,16,320]{3,2,1,0:T(8,128)(2,1)} %stack.12), calls=%async_computation | async-start | bytes 1769472 | tf_op jit(solution)/shard_map/all_to_all | solution.py:142
  31.5 1.9 %collective-permute-start.2 = (bf16[8,128]{1,0:T(8,128)(2,1)S(1)}, bf16[8,128]{1,0:T(8,128)(2,1)S(1)}, u32[]{:S(2)}, u32[]{:S(2)}) collective-permute-start(bf16[8,128]{1,0:T(8,128)(2,1)S(1)} %get-tuple-element.32), channel_id=1, source_target_pairs={{0,8},{8,16},{16,24},{24,32},{32,40},{40,48},{48,56},{56,64},{64,7... | collective-permute-start | bytes 6152 | tf_op jit(solution)/shard_map/ppermute | solution.py:14
  33.5 4.0 %collective-permute-start.3 = (bf16[8,128]{1,0:T(8,128)(2,1)S(1)}, bf16[8,128]{1,0:T(8,128)(2,1)S(1)}, u32[]{:S(2)}, u32[]{:S(2)}) collective-permute-start(bf16[8,128]{1,0:T(8,128)(2,1)S(1)} %get-tuple-element.31), channel_id=1, source_target_pairs={{0,16},{8,24},{16,32},{24,40},{32,48},{40,56},{48,64},{56,72},{64,... | collective-permute-start | bytes 6152 | tf_op jit(solution)/shard_map/ppermute | solution.py:14
  37.6 2.4 %collective-permute-done.2 = bf16[8,128]{1,0:T(8,128)(2,1)S(1)} collective-permute-done((bf16[8,128]{1,0:T(8,128)(2,1)S(1)}, bf16[8,128]{1,0:T(8,128)(2,1)S(1)}, u32[]{:S(2)}, u32[]{:S(2)}) %collective-permute-start.2) | collective-permute-done | bytes 2080 | tf_op jit(solution)/shard_map/ppermute | solution.py:14
  40.0 2.6 %collective-permute-done.3 = bf16[8,128]{1,0:T(8,128)(2,1)S(1)} collective-permute-done((bf16[8,128]{1,0:T(8,128)(2,1)S(1)}, bf16[8,128]{1,0:T(8,128)(2,1)S(1)}, u32[]{:S(2)}, u32[]{:S(2)}) %collective-permute-start.3) | collective-permute-done | bytes 2080 | tf_op jit(solution)/shard_map/ppermute | solution.py:14
  42.6 28.2 %all_gather.3 = bf16[64,640]{1,0:T(8,128)(2,1)S(1)} all-gather(bf16[8,640]{1,0:T(8,128)(2,1)S(1)} %bitcast.302), channel_id=1, replica_groups=mesh['tile'=64,'chan'=8] {'chan'}, dimensions={0}, use_global_device_ids=true | all-gather | bytes 92160 | tf_op jit(solution)/shard_map/all_gather | solution.py:161
  74.3 2.5 %collective-permute-start.4 = (bf16[64,2,60]{0,1,2:T(2,128)(2,1)S(1)}, bf16[64,2,60]{0,1,2:T(2,128)(2,1)S(1)}, u32[]{:S(2)}, u32[]{:S(2)}) collective-permute-start(bf16[64,2,60]{0,1,2:T(2,128)(2,1)S(1)} %get-tuple-element.29), channel_id=1, source_target_pairs={{0,1},{1,2},{2,3},{3,4},{4,5},{5,6},{6,7},{7,8},{8,9},{9,10},{10,1... | collective-permute-start | bytes 46088 | tf_op jit(solution)/shard_map/ppermute | solution.py:24
  76.8 5.6 %collective-permute-start.5 = (bf16[64,2,60]{0,1,2:T(2,128)(2,1)S(1)}, bf16[64,2,60]{0,1,2:T(2,128)(2,1)S(1)}, u32[]{:S(2)}, u32[]{:S(2)}) collective-permute-start(bf16[64,2,60]{0,1,2:T(2,128)(2,1)S(1)} %get-tuple-element.30), channel_id=1, source_target_pairs={{1,0},{2,1},{3,2},{4,3},{5,4},{6,5},{7,6},{8,7},{9,8},{10,9},{11,1... | collective-permute-start | bytes 46088 | tf_op jit(solution)/shard_map/ppermute | solution.py:25
  82.6 1.2 collective-permute-done.5
  84.0 1.4 gather_fusion.2
  85.9 2.0 %gather_fusion.3 = bf16[324,64,4]{1,2,0:T(4,128)(2,1)S(1)} fusion(bf16[64,4,324]{0,1,2:T(4,128)(2,1)S(1)} %pad_maximum_fusion.2, s32[1024]{0:T(1024)S(1)} %get-tuple-element.37), kind=kCustom, calls=%fused_computation.11 | custom fusion | bytes 333072 | tf_op jit(solution)/shard_map/jit(_take)/gather | solution.py:101
  94.0 1.1 fusion.18
  96.0 2.2 %collective-permute-start.6 = (bf16[128,2,60]{0,1,2:T(2,128)(2,1)S(1)}, bf16[128,2,60]{0,1,2:T(2,128)(2,1)S(1)}, u32[]{:S(2)}, u32[]{:S(2)}) collective-permute-start(bf16[128,2,60]{0,1,2:T(2,128)(2,1)S(1)} %get-tuple-element.27), channel_id=1, source_target_pairs={{0,1},{1,2},{2,3},{3,4},{4,5},{5,6},{6,7},{7,8},{8,9},{9,10},{10,1... | collective-permute-start | bytes 92168 | tf_op jit(solution)/shard_map/ppermute | solution.py:24
  98.1 6.3 %collective-permute-start.7 = (bf16[128,2,60]{0,1,2:T(2,128)(2,1)S(1)}, bf16[128,2,60]{0,1,2:T(2,128)(2,1)S(1)}, u32[]{:S(2)}, u32[]{:S(2)}) collective-permute-start(bf16[128,2,60]{0,1,2:T(2,128)(2,1)S(1)} %get-tuple-element.28), channel_id=1, source_target_pairs={{1,0},{2,1},{3,2},{4,3},{5,4},{6,5},{7,6},{8,7},{9,8},{10,9},{11,1... | collective-permute-start | bytes 92168 | tf_op jit(solution)/shard_map/ppermute | solution.py:25
  104.5 1.3 collective-permute-done.7
  106.0 1.4 gather_fusion.7
  107.9 2.0 %gather_fusion.8 = bf16[324,128,4]{1,2,0:T(4,128)(2,1)S(1)} fusion(bf16[128,4,324]{0,1,2:T(4,128)(2,1)S(1)} %copy.253, s32[1024]{0:T(1024)S(1)} %get-tuple-element.37), kind=kCustom, calls=%fused_computation.3.clone | custom fusion | bytes 664848 | tf_op jit(solution)/shard_map/jit(_take)/gather | solution.py:101
  114.1 1.1 fusion.21
  116.1 2.1 %collective-permute-start.8 = (bf16[128,2,60]{0,1,2:T(2,128)(2,1)S(1)}, bf16[128,2,60]{0,1,2:T(2,128)(2,1)S(1)}, u32[]{:S(2)}, u32[]{:S(2)}) collective-permute-start(bf16[128,2,60]{0,1,2:T(2,128)(2,1)S(1)} %get-tuple-element.25), channel_id=1, source_target_pairs={{0,1},{1,2},{2,3},{3,4},{4,5},{5,6},{6,7},{7,8},{8,9},{9,10},{10,1... | collective-permute-start | bytes 92168 | tf_op jit(solution)/shard_map/ppermute | solution.py:24
  118.2 6.2 %collective-permute-start.9 = (bf16[128,2,60]{0,1,2:T(2,128)(2,1)S(1)}, bf16[128,2,60]{0,1,2:T(2,128)(2,1)S(1)}, u32[]{:S(2)}, u32[]{:S(2)}) collective-permute-start(bf16[128,2,60]{0,1,2:T(2,128)(2,1)S(1)} %get-tuple-element.26), channel_id=1, source_target_pairs={{1,0},{2,1},{3,2},{4,3},{5,4},{6,5},{7,6},{8,7},{9,8},{10,9},{11,1... | collective-permute-start | bytes 92168 | tf_op jit(solution)/shard_map/ppermute | solution.py:25
  124.4 1.5 %collective-permute-done.9 = bf16[128,2,60]{0,1,2:T(2,128)(2,1)S(1)} collective-permute-done((bf16[128,2,60]{0,1,2:T(2,128)(2,1)S(1)}, bf16[128,2,60]{0,1,2:T(2,128)(2,1)S(1)}, u32[]{:S(2)}, u32[]{:S(2)}) %collective-permute-start.9) | collective-permute-done | bytes 30752 | tf_op jit(solution)/shard_map/ppermute | solution.py:25
  126.1 1.4 gather_fusion.10
  128.1 2.0 %gather_fusion.11 = bf16[324,128,4]{1,2,0:T(4,128)(2,1)S(1)} fusion(bf16[128,4,324]{0,1,2:T(4,128)(2,1)S(1)} %copy.267, s32[1024]{0:T(1024)S(1)} %get-tuple-element.37), kind=kCustom, calls=%fused_computation.7.clone | custom fusion | bytes 664848 | tf_op jit(solution)/shard_map/jit(_take)/gather | solution.py:101
  134.2 1.1 fusion.24
  135.5 17.6 %all_to_all.23 = bf16[128,4,256]{2,1,0:T(4,128)(2,1)S(1)} all-to-all(bf16[128,4,256]{2,1,0:T(4,128)(2,1)S(1)} %copy.278), channel_id=1, replica_groups=mesh['tile'=64,'chan'=8] {'chan'}, dimensions={0} | all-to-all | bytes 524288 | tf_op jit(solution)/shard_map/all_to_all | solution.py:185
  153.2 0.8 copy.281
  (149 shorter events, 26.0 us)
Async XLA Ops:
  0.0 28.9 %copy-start = (s32[32,8]{0,1:T(8,128)S(1)}, s32[32,8]{0,1:T(8,128)}, u32[]{:S(2)}) copy-start(s32[32,8]{0,1:T(8,128)} %param.36) | copy-start | bytes 3076
  0.0 21.1 %copy-start.3 = (bf16[9,16,64]{2,1,0:T(8,128)(2,1)S(1)}, bf16[9,16,64]{2,1,0:T(8,128)(2,1)}, u32[]{:S(2)}) copy-start(bf16[9,16,64]{2,1,0:T(8,128)(2,1)} %param.37) | copy-start | bytes 55300
  0.0 21.1 %copy-start.2 = (bf16[9,16,128]{2,1,0:T(8,128)(2,1)S(1)}, bf16[9,16,128]{2,1,0:T(8,128)(2,1)}, u32[]{:S(2)}) copy-start(bf16[9,16,128]{2,1,0:T(8,128)(2,1)} %param.38) | copy-start | bytes 110596
  0.0 21.1 %copy-start.1 = (bf16[9,16,128]{2,1,0:T(8,128)(2,1)S(1)}, bf16[9,16,128]{2,1,0:T(8,128)(2,1)}, u32[]{:S(2)}) copy-start(bf16[9,16,128]{2,1,0:T(8,128)(2,1)} %param.39) | copy-start | bytes 110596
  3.4 24.7 %copy-start.7 = (s32[68]{0:T(128)S(1)}, s32[68]{0:T(128)}, u32[]{:S(2)}) copy-start(s32[68]{0:T(128)} %constant.310) | copy-start | bytes 820
  3.4 24.7 %copy-start.4 = (s32[32,8]{0,1:T(8,128)S(1)}, s32[32,8]{0,1:T(8,128)}, u32[]{:S(2)}) copy-start(s32[32,8]{0,1:T(8,128)} %param.35) | copy-start | bytes 3076
  3.4 26.3 %copy-start.6 = (s32[68]{0:T(128)S(1)}, s32[68]{0:T(128)}, u32[]{:S(2)}) copy-start(s32[68]{0:T(128)} %constant.243) | copy-start | bytes 820
  3.5 30.0 %copy-start.8 = (s32[60]{0:T(128)S(1)}, s32[60]{0:T(128)}, u32[]{:S(2)}) copy-start(s32[60]{0:T(128)} %constant.221.clone) | copy-start | bytes 724
  5.6 25.8 %collective-permute-start = (bf16[8,128]{1,0:T(8,128)(2,1)S(1)}, bf16[8,128]{1,0:T(8,128)(2,1)S(1)}, u32[]{:S(2)}, u32[]{:S(2)}) collective-permute-start(bf16[8,128]{1,0:T(8,128)(2,1)S(1)} %get-tuple-element.35), channel_id=1, source_target_pairs={{0,496},{8,504},{16,0},{24,8},{32,16},{40,24},{48,32},{56,40},{64,... | collective-permute-start | bytes 6152 | tf_op jit(solution)/shard_map/ppermute | solution.py:14
  18.6 12.9 %collective-permute-start.1 = (bf16[8,128]{1,0:T(8,128)(2,1)S(1)}, bf16[8,128]{1,0:T(8,128)(2,1)S(1)}, u32[]{:S(2)}, u32[]{:S(2)}) collective-permute-start(bf16[8,128]{1,0:T(8,128)(2,1)S(1)} %get-tuple-element.34), channel_id=1, source_target_pairs={{0,504},{8,0},{16,8},{24,16},{32,24},{40,32},{48,40},{56,48},{64,5... | collective-permute-start | bytes 6152 | tf_op jit(solution)/shard_map/ppermute | solution.py:14
  22.2 65.9 %all-to-all-start = ((bf16[8,9,16,320]{3,2,1,0:T(8,128)(2,1)}), bf16[8,9,16,320]{3,2,1,0:T(8,128)(2,1)S(1)}, u32[]{:S(2)}, u32[]{:S(2)}) async-start(bf16[8,9,16,320]{3,2,1,0:T(8,128)(2,1)} %stack.12), calls=%async_computation | async-start | bytes 1769472 | tf_op jit(solution)/shard_map/all_to_all | solution.py:142
  31.5 8.5 %collective-permute-start.2 = (bf16[8,128]{1,0:T(8,128)(2,1)S(1)}, bf16[8,128]{1,0:T(8,128)(2,1)S(1)}, u32[]{:S(2)}, u32[]{:S(2)}) collective-permute-start(bf16[8,128]{1,0:T(8,128)(2,1)S(1)} %get-tuple-element.32), channel_id=1, source_target_pairs={{0,8},{8,16},{16,24},{24,32},{32,40},{40,48},{48,56},{56,64},{64,7... | collective-permute-start | bytes 6152 | tf_op jit(solution)/shard_map/ppermute | solution.py:14
  33.5 9.1 %collective-permute-start.3 = (bf16[8,128]{1,0:T(8,128)(2,1)S(1)}, bf16[8,128]{1,0:T(8,128)(2,1)S(1)}, u32[]{:S(2)}, u32[]{:S(2)}) collective-permute-start(bf16[8,128]{1,0:T(8,128)(2,1)S(1)} %get-tuple-element.31), channel_id=1, source_target_pairs={{0,16},{8,24},{16,32},{24,40},{32,48},{40,56},{48,64},{56,72},{64,... | collective-permute-start | bytes 6152 | tf_op jit(solution)/shard_map/ppermute | solution.py:14
  71.4 11.0 %copy-start.5 = (s32[324]{0:T(512)S(1)}, s32[324]{0:T(512)}, u32[]{:S(2)}) copy-start(s32[324]{0:T(512)} %constant.224.clone) | copy-start | bytes 3892
  74.3 8.3 %collective-permute-start.4 = (bf16[64,2,60]{0,1,2:T(2,128)(2,1)S(1)}, bf16[64,2,60]{0,1,2:T(2,128)(2,1)S(1)}, u32[]{:S(2)}, u32[]{:S(2)}) collective-permute-start(bf16[64,2,60]{0,1,2:T(2,128)(2,1)S(1)} %get-tuple-element.29), channel_id=1, source_target_pairs={{0,1},{1,2},{2,3},{3,4},{4,5},{5,6},{6,7},{7,8},{8,9},{9,10},{10,1... | collective-permute-start | bytes 46088 | tf_op jit(solution)/shard_map/ppermute | solution.py:24
  76.8 7.0 %collective-permute-start.5 = (bf16[64,2,60]{0,1,2:T(2,128)(2,1)S(1)}, bf16[64,2,60]{0,1,2:T(2,128)(2,1)S(1)}, u32[]{:S(2)}, u32[]{:S(2)}) collective-permute-start(bf16[64,2,60]{0,1,2:T(2,128)(2,1)S(1)} %get-tuple-element.30), channel_id=1, source_target_pairs={{1,0},{2,1},{3,2},{4,3},{5,4},{6,5},{7,6},{8,7},{9,8},{10,9},{11,1... | collective-permute-start | bytes 46088 | tf_op jit(solution)/shard_map/ppermute | solution.py:25
  96.0 8.5 %collective-permute-start.6 = (bf16[128,2,60]{0,1,2:T(2,128)(2,1)S(1)}, bf16[128,2,60]{0,1,2:T(2,128)(2,1)S(1)}, u32[]{:S(2)}, u32[]{:S(2)}) collective-permute-start(bf16[128,2,60]{0,1,2:T(2,128)(2,1)S(1)} %get-tuple-element.27), channel_id=1, source_target_pairs={{0,1},{1,2},{2,3},{3,4},{4,5},{5,6},{6,7},{7,8},{8,9},{9,10},{10,1... | collective-permute-start | bytes 92168 | tf_op jit(solution)/shard_map/ppermute | solution.py:24
  98.1 7.6 %collective-permute-start.7 = (bf16[128,2,60]{0,1,2:T(2,128)(2,1)S(1)}, bf16[128,2,60]{0,1,2:T(2,128)(2,1)S(1)}, u32[]{:S(2)}, u32[]{:S(2)}) collective-permute-start(bf16[128,2,60]{0,1,2:T(2,128)(2,1)S(1)} %get-tuple-element.28), channel_id=1, source_target_pairs={{1,0},{2,1},{3,2},{4,3},{5,4},{6,5},{7,6},{8,7},{9,8},{10,9},{11,1... | collective-permute-start | bytes 92168 | tf_op jit(solution)/shard_map/ppermute | solution.py:25
  116.1 8.3 %collective-permute-start.8 = (bf16[128,2,60]{0,1,2:T(2,128)(2,1)S(1)}, bf16[128,2,60]{0,1,2:T(2,128)(2,1)S(1)}, u32[]{:S(2)}, u32[]{:S(2)}) collective-permute-start(bf16[128,2,60]{0,1,2:T(2,128)(2,1)S(1)} %get-tuple-element.25), channel_id=1, source_target_pairs={{0,1},{1,2},{2,3},{3,4},{4,5},{5,6},{6,7},{7,8},{8,9},{9,10},{10,1... | collective-permute-start | bytes 92168 | tf_op jit(solution)/shard_map/ppermute | solution.py:24
  118.2 7.8 %collective-permute-start.9 = (bf16[128,2,60]{0,1,2:T(2,128)(2,1)S(1)}, bf16[128,2,60]{0,1,2:T(2,128)(2,1)S(1)}, u32[]{:S(2)}, u32[]{:S(2)}) collective-permute-start(bf16[128,2,60]{0,1,2:T(2,128)(2,1)S(1)} %get-tuple-element.26), channel_id=1, source_target_pairs={{1,0},{2,1},{3,2},{4,3},{5,4},{6,5},{7,6},{8,7},{9,8},{10,9},{11,1... | collective-permute-start | bytes 92168 | tf_op jit(solution)/shard_map/ppermute | solution.py:25
